TPU v7x, 32 devices: a whole 2x2x4 slice. The times are simulated.
32 devices in a mesh: dp: 4 (over z), pipe: 2 (over core), expert: 4 (over y, x).
Axes of the slice: x: 2, y: 2, z: 4, core: 2. Of those that a mesh axis runs over, the one named last changes fastest.
Arguments:
- tokens: bfloat16 [2, 96, 3072], P(None, 'expert'), may hold values from -6 to 6
- expert_ids: int32 [2, 2, 96, 2], P('pipe', None, 'expert'), may hold values from 0 to 3, all different within a row; in each aligned block of 24 rows (0 to 23, 24 to 47, ..., all dimensions but the last counted through in order) at most 16 rows name the same one
- gates: float32 [2, 2, 96, 2], P('pipe', None, 'expert'), may hold values from 0.1 to 1
- w_gate: bfloat16 [2, 4, 3072, 704], P('pipe', 'expert', None, 'dp'), may hold values from -0.109375 to 0.109375
- w_up: bfloat16 [2, 4, 3072, 704], P('pipe', 'expert', None, 'dp'), may hold values from -0.109375 to 0.109375
- w_down: bfloat16 [2, 4, 704, 3072], P('pipe', 'expert', 'dp'), may hold values from -0.3125 to 0.3125
Outputs:
- layer_out: bfloat16 [2, 2, 96, 3072], P('pipe', None, 'expert', 'dp')
Inputs may be any that keep to these rules, and one draw needn't show every extreme that they name: `expert_ids`: each token names 2 different experts in each layer. Among the tokens of one index of expert in one layer and micro-batch (aligned blocks of 24 tokens) no expert is named by more than 16 tokens, and in some block an expert is named by exactly 16.
All inputs are finite; a program needn't handle non-finite values.
Results may differ from a plain program's by a relative error of at most 0.0052.
Values may be sent and summed in bfloat16 or wider, within the bound.
No kernel may reach another device: no remote copies, remote signals or barrier semaphores. Data moves between devices by JAX's collectives and lax.ppermute only.
A program may use at most 64 MiB of HBM per device.

v0:
```python
import jax
import jax.numpy as jnp
from jax import lax
from jax.sharding import PartitionSpec as P

TOP = 2
CAP = 16


def passed_along(value, axis, by):
    length = lax.axis_size(axis)
    pairs = [(i, i + by) for i in range(length) if 0 <= i + by < length]
    return lax.ppermute(value, axis, pairs)


def build_maps(route_ids, route_gates, experts, rows_all):
    flat_ids = route_ids.reshape(-1)
    onehot = (flat_ids[:, None] == jnp.arange(experts, dtype=jnp.int32)[None, :]).astype(jnp.int32)
    before = jnp.cumsum(onehot, axis=0) - onehot
    placed = flat_ids * CAP + jnp.sum(before * onehot, axis=1)
    matches = jnp.arange(rows_all, dtype=jnp.int32)[:, None] == placed[None, :]
    dispatch_map = jnp.sum(matches.astype(jnp.float32).reshape(rows_all, -1, TOP), axis=2).astype(
        jnp.bfloat16
    )
    combine_map = jnp.sum(
        jnp.where(matches, route_gates.reshape(-1)[None, :], 0.0).reshape(rows_all, -1, TOP), axis=2
    )
    return (dispatch_map, combine_map)


def per_device(tokens, expert_ids, gates, w_gate, w_up, w_down):
    experts = lax.axis_size("expert")
    dp_size = lax.axis_size("dp")
    sections = lax.axis_size("pipe")
    micro_count = tokens.shape[0]
    tok_rows = tokens.shape[1]
    model_width = tokens.shape[2]
    unit_count = w_gate.shape[3]
    columns = model_width // dp_size
    rows_all = experts * CAP
    gate_local = w_gate[0, 0]
    up_local = w_up[0, 0]
    down_local = w_down[0, 0]
    section = lax.axis_index("pipe")
    is_first = section == 0
    column_start = lax.axis_index("dp") * columns
    outputs = jnp.zeros((1, micro_count, tok_rows, columns), jnp.bfloat16)
    carried = jnp.zeros((tok_rows, model_width), jnp.bfloat16)
    turns = micro_count + sections - 1
    for moment in range(turns):
        offset_micro = moment - section
        in_window = (offset_micro >= 0) & (offset_micro < micro_count)
        micro_index = jnp.clip(offset_micro, 0, micro_count - 1)
        own_rows = tokens[min(moment, micro_count - 1)]
        route_ids = lax.dynamic_index_in_dim(expert_ids[0], micro_index, 0, keepdims=False)
        route_gates = lax.dynamic_index_in_dim(gates[0], micro_index, 0, keepdims=False)
        dispatch_map, combine_map = build_maps(route_ids, route_gates, experts, rows_all)
        current = jnp.where(is_first, own_rows, carried)
        current_cols = lax.dynamic_slice_in_dim(current, column_start, columns, 1)
        outgoing = jnp.dot(dispatch_map, current, preferred_element_type=jnp.float32)
        outgoing = outgoing.astype(jnp.bfloat16).reshape(experts, CAP, model_width)
        arrived = lax.all_to_all(outgoing, "expert", split_axis=0, concat_axis=0, tiled=True)
        flat_rows = arrived.reshape(-1, model_width)
        squares = jnp.mean(jnp.square(flat_rows.astype(jnp.float32)), axis=1, keepdims=True)
        inv_rms = lax.rsqrt(squares + 1e-05)
        gate_act = jnp.dot(flat_rows, gate_local, preferred_element_type=jnp.float32) * inv_rms
        up_act = jnp.dot(flat_rows, up_local, preferred_element_type=jnp.float32) * inv_rms
        hidden_rows = (jax.nn.silu(gate_act) * up_act).astype(jnp.bfloat16)
        hidden = hidden_rows.reshape(arrived.shape[0], arrived.shape[1], unit_count)
        hidden = hidden.reshape(rows_all, unit_count)
        summed = lax.psum_scatter(
            lax.dot_general(
                down_local, hidden, (((0,), (1,)), ((), ())), preferred_element_type=jnp.float32
            ),
            "dp",
            scatter_dimension=0,
            tiled=True,
        )
        shares = summed.astype(jnp.bfloat16).reshape(columns, experts, CAP)
        returned = lax.all_to_all(
            shares, "expert", split_axis=1, concat_axis=1, tiled=True
        ).reshape(columns, rows_all)
        mixed = lax.dot_general(
            combine_map,
            returned.astype(jnp.float32),
            (((0,), (1,)), ((), ())),
            precision=lax.Precision.HIGHEST,
            preferred_element_type=jnp.float32,
        )
        new_cols = (current_cols.astype(jnp.float32) + mixed).astype(jnp.bfloat16)
        updated = lax.dynamic_update_slice_in_dim(outputs, new_cols[None, None], micro_index, 1)
        outputs = jnp.where(in_window, updated, outputs)
        if moment + 1 < turns:
            full_rows = lax.all_gather(new_cols, "dp", axis=1, tiled=True)
            carried = passed_along(full_rows, "pipe", 1)
    return outputs


def solution(mesh):
    return jax.shard_map(
        per_device,
        mesh=mesh,
        in_specs=(
            P(None, "expert", None),
            P("pipe", None, "expert", None),
            P("pipe", None, "expert", None),
            P("pipe", "expert", None, "dp"),
            P("pipe", "expert", None, "dp"),
            P("pipe", "expert", "dp", None),
        ),
        out_specs=P("pipe", None, "expert", "dp"),
        check_vma=False,
    )
```

profile of v0, /device:TPU:0, one launch (start us, length us, event | category | flops | bytes accessed | tf_op | source)
XLA Modules:
  0.0 198.9 jit_solution(14078611586446322383)
XLA Ops:
  10.1 12.1 %all_to_all.30 = bf16[4,16,3072]{2,1,0:T(8,128)(2,1)S(1)} all-to-all(bf16[4,16,3072]{2,1,0:T(8,128)(2,1)S(1)} %bitcast.104), channel_id=1, replica_groups=mesh['dp'=4,'pipe'=2,'expert'=4] {'expert'}, dimensions={0} | all-to-all | bytes 786432 | tf_op jit(solution)/shard_map/all_to_all | solution.py:62
  23.2 1.5 convolution_multiply_fusion.5
  24.8 2.8 %convolution_bitcast_fusion.2 = f32[3072,64]{0,1:T(8,128)} fusion(bf16[64,3072]{1,0:T(8,128)(2,1)} %bitcast.99, bf16[1,1,176,3072]{3,2,1,0:T(8,128)(2,1)S(1)} %copy-done, bf16[1,1,3072,176]{2,3,1,0:T(8,128)(2,1)S(1)} %copy-done.2, f32[64,176]{1,0:T(8,128)S(1)} %convolution_multiply_fusion.5, f32[64]{0:T(128)S(1)} %rsqrt.34), kind=kOutput, calls=%fused_computation.2 | convolution fusion | flops 138490880 | bytes 3387648 | tf_op jit(solution)/shard_map/dot_general | solution.py:72
  28.7 22.1 %reduce-scatter.4.cloned.1.call-done = f32[768,64]{0,1:T(8,128)} async-done(((f32[3072,64]{0,1:T(8,128)}), f32[768,64]{0,1:T(8,128)}) %reduce-scatter.4.cloned.1.call-update) | async-done | bytes 196624 | tf_op jit(solution)/shard_map/reduce_scatter | solution.py:71
  50.8 1.6 convert_element_type.101
  52.4 3.6 %all-to-all-start.1 = ((bf16[768,4,16]{0,2,1:T(8,128)(2,1)}), bf16[768,4,16]{0,2,1:T(8,128)(2,1)S(1)}, u32[]{:S(2)}, u32[]{:S(2)}) async-start(bf16[768,4,16]{0,2,1:T(8,128)(2,1)} %bitcast.110), calls=%async_computation.2 | async-start | bytes 196608 | tf_op jit(solution)/shard_map/all_to_all | solution.py:80
  56.4 4.6 %all-to-all-done.1 = bf16[768,4,16]{0,2,1:T(8,128)(2,1)S(1)} async-done(((bf16[768,4,16]{0,2,1:T(8,128)(2,1)}), bf16[768,4,16]{0,2,1:T(8,128)(2,1)S(1)}, u32[]{:S(2)}, u32[]{:S(2)}) %all-to-all-start.1) | async-done | bytes 98336 | tf_op jit(solution)/shard_map/all_to_all | solution.py:80
  61.2 13.5 %all_gather.6 = bf16[24,3072]{1,0:T(8,128)(2,1)S(1)} all-gather(bf16[24,768]{1,0:T(8,128)(2,1)S(1)} %get-tuple-element.20), channel_id=1, replica_groups=mesh['dp'=4,'pipe'=2,'expert'=4] {'dp'}, dimensions={1}, use_global_device_ids=true | all-gather | bytes 184320 | tf_op jit(solution)/shard_map/all_gather | solution.py:94
  78.1 10.3 %all_to_all.31 = bf16[4,16,3072]{2,1,0:T(8,128)(2,1)S(1)} all-to-all(bf16[4,16,3072]{2,1,0:T(8,128)(2,1)S(1)} %bitcast.105), channel_id=1, replica_groups=mesh['dp'=4,'pipe'=2,'expert'=4] {'expert'}, dimensions={0} | all-to-all | bytes 786432 | tf_op jit(solution)/shard_map/all_to_all | solution.py:62
  90.9 2.8 %convolution_bitcast_fusion.1 = f32[3072,64]{0,1:T(8,128)} fusion(bf16[64,3072]{1,0:T(8,128)(2,1)} %bitcast.101, bf16[1,1,176,3072]{3,2,1,0:T(8,128)(2,1)S(1)} %copy-done, bf16[1,1,3072,176]{2,3,1,0:T(8,128)(2,1)S(1)} %copy-done.2, f32[64,176]{1,0:T(8,128)S(1)} %convolution_multiply_fusion.3, f32[64]{0:T(128)S(1)} %rsqrt.36), kind=kOutput, calls=%fused_computation.1 | convolution fusion | flops 138490880 | bytes 3387648 | tf_op jit(solution)/shard_map/dot_general | solution.py:72
  93.8 21.2 %reduce-scatter.6.cloned.1.call-done = f32[768,64]{0,1:T(8,128)} async-done(((f32[3072,64]{0,1:T(8,128)}), f32[768,64]{0,1:T(8,128)}) %reduce-scatter.6.cloned.1.call-update) | async-done | bytes 196624 | tf_op jit(solution)/shard_map/reduce_scatter | solution.py:71
  115.1 1.6 convert_element_type.110
  116.6 3.7 %all-to-all-start.3 = ((bf16[768,4,16]{0,2,1:T(8,128)(2,1)}), bf16[768,4,16]{0,2,1:T(8,128)(2,1)S(1)}, u32[]{:S(2)}, u32[]{:S(2)}) async-start(bf16[768,4,16]{0,2,1:T(8,128)(2,1)} %bitcast.111), calls=%async_computation.5 | async-start | bytes 196608 | tf_op jit(solution)/shard_map/all_to_all | solution.py:80
  120.3 4.9 %all-to-all-done.3 = bf16[768,4,16]{0,2,1:T(8,128)(2,1)S(1)} async-done(((bf16[768,4,16]{0,2,1:T(8,128)(2,1)}), bf16[768,4,16]{0,2,1:T(8,128)(2,1)S(1)}, u32[]{:S(2)}, u32[]{:S(2)}) %all-to-all-start.3) | async-done | bytes 98336 | tf_op jit(solution)/shard_map/all_to_all | solution.py:80
  125.2 1.6 fusion.38
  126.8 13.4 %all_gather.7 = bf16[24,3072]{1,0:T(8,128)(2,1)S(1)} all-gather(bf16[24,768]{1,0:T(8,128)(2,1)S(1)} %get-tuple-element.12), channel_id=1, replica_groups=mesh['dp'=4,'pipe'=2,'expert'=4] {'dp'}, dimensions={1}, use_global_device_ids=true | all-gather | bytes 184320 | tf_op jit(solution)/shard_map/all_gather | solution.py:94
  143.7 10.3 %all_to_all.32 = bf16[4,16,3072]{2,1,0:T(8,128)(2,1)S(1)} all-to-all(bf16[4,16,3072]{2,1,0:T(8,128)(2,1)S(1)} %bitcast.106), channel_id=1, replica_groups=mesh['dp'=4,'pipe'=2,'expert'=4] {'expert'}, dimensions={0} | all-to-all | bytes 786432 | tf_op jit(solution)/shard_map/all_to_all | solution.py:62
  155.0 1.5 convolution_multiply_fusion.1
  156.5 2.9 %convolution_bitcast_fusion = f32[3072,64]{0,1:T(8,128)} fusion(bf16[64,3072]{1,0:T(8,128)(2,1)} %bitcast.103, bf16[1,1,176,3072]{3,2,1,0:T(8,128)(2,1)S(1)} %copy-done, bf16[1,1,3072,176]{2,3,1,0:T(8,128)(2,1)S(1)} %copy-done.2, f32[64,176]{1,0:T(8,128)S(1)} %convolution_multiply_fusion.1, f32[64]{0:T(128)S(1)} %rsqrt.38), kind=kOutput, calls=%fused_computation | convolution fusion | flops 138490880 | bytes 3387648 | tf_op jit(solution)/shard_map/dot_general | solution.py:72
  159.3 21.3 %reduce-scatter.8.cloned.1.call-done = f32[768,64]{0,1:T(8,128)} async-done(((f32[3072,64]{0,1:T(8,128)}), f32[768,64]{0,1:T(8,128)}) %reduce-scatter.8.cloned.1.call-update) | async-done | bytes 196624 | tf_op jit(solution)/shard_map/reduce_scatter | solution.py:71
  180.7 1.6 convert_element_type.119
  182.2 3.7 %all-to-all-start.5 = ((bf16[768,4,16]{0,2,1:T(8,128)(2,1)}), bf16[768,4,16]{0,2,1:T(8,128)(2,1)S(1)}, u32[]{:S(2)}, u32[]{:S(2)}) async-start(bf16[768,4,16]{0,2,1:T(8,128)(2,1)} %bitcast.27), calls=%async_computation.8 | async-start | bytes 196608 | tf_op jit(solution)/shard_map/all_to_all | solution.py:80
  185.9 4.9 %all-to-all-done.5 = bf16[768,4,16]{0,2,1:T(8,128)(2,1)S(1)} async-done(((bf16[768,4,16]{0,2,1:T(8,128)(2,1)}), bf16[768,4,16]{0,2,1:T(8,128)(2,1)S(1)}, u32[]{:S(2)}, u32[]{:S(2)}) %all-to-all-start.5) | async-done | bytes 98336 | tf_op jit(solution)/shard_map/all_to_all | solution.py:80
  190.8 1.6 fusion.37
  (70 shorter events, 16.6 us)
Async XLA Ops:
  6.5 18.2 %copy-start = (bf16[1,1,176,3072]{3,2,1,0:T(8,128)(2,1)S(1)}, bf16[1,1,176,3072]{3,2,1,0:T(8,128)(2,1)}, u32[]{:S(2)}) copy-start(bf16[1,1,176,3072]{3,2,1,0:T(8,128)(2,1)} %param.11) | copy-start | bytes 3244036
  6.5 44.3 %reduce-scatter.4.cloned.1.call-start = ((), (), s32[]{:S(2)}) async-start(), calls=%async_computation.9 | async-start | bytes 983040 | tf_op jit(solution)/shard_map/reduce_scatter | solution.py:71
  7.6 15.6 %copy-start.1 = (bf16[1,1,3072,176]{2,3,1,0:T(8,128)(2,1)S(1)}, bf16[1,1,3072,176]{2,3,1,0:T(8,128)(2,1)}, u32[]{:S(2)}) copy-start(bf16[1,1,3072,176]{2,3,1,0:T(8,128)(2,1)} %param.9) | copy-start | bytes 3244036
  22.2 0.7 copy-start.3
  23.0 1.8 copy-start.2
  52.4 8.6 %all-to-all-start.1 = ((bf16[768,4,16]{0,2,1:T(8,128)(2,1)}), bf16[768,4,16]{0,2,1:T(8,128)(2,1)S(1)}, u32[]{:S(2)}, u32[]{:S(2)}) async-start(bf16[768,4,16]{0,2,1:T(8,128)(2,1)} %bitcast.110), calls=%async_computation.2 | async-start | bytes 196608 | tf_op jit(solution)/shard_map/all_to_all | solution.py:80
  56.0 59.0 %reduce-scatter.6.cloned.1.call-start = ((), (), s32[]{:S(2)}) async-start(), calls=%async_computation.10 | async-start | bytes 983040 | tf_op jit(solution)/shard_map/reduce_scatter | solution.py:71
  61.2 16.7 %copy-start.6 = (bf16[1,2,24,768]{3,2,1,0:T(8,128)(2,1)}, bf16[1,2,24,768]{3,2,1,0:T(8,128)(2,1)S(1)}, u32[]{:S(2)}) copy-start(bf16[1,2,24,768]{3,2,1,0:T(8,128)(2,1)S(1)} %get-tuple-element.19) | copy-start | bytes 221188
  74.6 2.3 %collective-permute-start = (bf16[24,3072]{1,0:T(8,128)(2,1)S(1)}, bf16[24,3072]{1,0:T(8,128)(2,1)S(1)}, u32[]{:S(2)}, u32[]{:S(2)}) collective-permute-start(bf16[24,3072]{1,0:T(8,128)(2,1)S(1)} %all_gather.6), channel_id=1, source_target_pairs={{0,4},{1,5},{2,6},{3,7},{8,12},{9,13},{10,14},{11,15},{16,20},{17,... | collective-permute-start | bytes 442376 | tf_op jit(solution)/shard_map/ppermute | solution.py:13
  88.5 0.7 copy-start.4
  116.6 8.6 %all-to-all-start.3 = ((bf16[768,4,16]{0,2,1:T(8,128)(2,1)}), bf16[768,4,16]{0,2,1:T(8,128)(2,1)S(1)}, u32[]{:S(2)}, u32[]{:S(2)}) async-start(bf16[768,4,16]{0,2,1:T(8,128)(2,1)} %bitcast.111), calls=%async_computation.5 | async-start | bytes 196608 | tf_op jit(solution)/shard_map/all_to_all | solution.py:80
  120.3 60.4 %reduce-scatter.8.cloned.1.call-start = ((), (), s32[]{:S(2)}) async-start(), calls=%async_computation.11 | async-start | bytes 983040 | tf_op jit(solution)/shard_map/reduce_scatter | solution.py:71
  140.2 2.3 %collective-permute-start.1 = (bf16[24,3072]{1,0:T(8,128)(2,1)S(1)}, bf16[24,3072]{1,0:T(8,128)(2,1)S(1)}, u32[]{:S(2)}, u32[]{:S(2)}) collective-permute-start(bf16[24,3072]{1,0:T(8,128)(2,1)S(1)} %all_gather.7), channel_id=1, source_target_pairs={{0,4},{1,5},{2,6},{3,7},{8,12},{9,13},{10,14},{11,15},{16,20},{17,... | collective-permute-start | bytes 442376 | tf_op jit(solution)/shard_map/ppermute | solution.py:13
  154.0 0.7 copy-start.5
  182.2 8.6 %all-to-all-start.5 = ((bf16[768,4,16]{0,2,1:T(8,128)(2,1)}), bf16[768,4,16]{0,2,1:T(8,128)(2,1)S(1)}, u32[]{:S(2)}, u32[]{:S(2)}) async-start(bf16[768,4,16]{0,2,1:T(8,128)(2,1)} %bitcast.27), calls=%async_computation.8 | async-start | bytes 196608 | tf_op jit(solution)/shard_map/all_to_all | solution.py:80
Sparse Core Ops, SparseCore 0:
  27.8 23.0 reduce-scatter.3
  93.9 21.0 reduce-scatter.5
  159.5 21.1 reduce-scatter.7
where the time goes:
time: 200 us; the launch traced here: 199 us
  waiting for transfers between devices  81 us (40%)
  blocking collectives  59.6 us (30%)
  matrix products  17.2 us (9%)
  starting transfers between devices  13.5 us (7%)
  between operations  13.3 us (7%)
  other arithmetic  9.16 us (5%)
  local copies, waits for them, and re-layouts  5.17 us (3%)
    reduce_scatter x3, waiting for transfers between devices, per_device(): lax.psum_scatter(lax.dot_general(down_local, hidden, (((0,), (1,)), ((),...  64.7 us
    all_to_all x3, blocking collectives, per_device(): lax.all_to_all(outgoing, 'expert', split_axis=0, concat_axis=0, tiled=True)  32.7 us
    all_gather x2, blocking collectives, per_device(): full_rows = lax.all_gather(new_cols, 'dp', axis=1, tiled=True)  26.9 us
    all_to_all x3, waiting for transfers between devices, per_device(): lax.all_to_all(shares, 'expert', split_axis=1, concat_axis=1, tiled=True)  14.4 us
    all_to_all x3, starting transfers between devices, per_device(): lax.all_to_all(shares, 'expert', split_axis=1, concat_axis=1, tiled=True)  11 us
    dot_general x3, matrix products, per_device(): lax.dot_general(down_local, hidden, (((0,), (1,)), ((), ())), preferred_e...  8.54 us
    convert_element_type x3, other arithmetic, per_device(): shares = summed.astype(jnp.bfloat16).reshape(columns, experts, CAP)  4.68 us
    dot_general x3, matrix products, per_device(): jnp.dot(flat_rows, gate_local, preferred_element_type=jnp.float32) * inv_rms  4.54 us
  transfers between devices with their start and end apart: 8, of which 8 were waited for; matrix products, arithmetic and copies ran while one was open for 1% of the time, Pallas kernels for 0%

commit v1 on v0

--- a/solution.py
+++ b/solution.py
@@ -91,7 +91,27 @@
         updated = lax.dynamic_update_slice_in_dim(outputs, new_cols[None, None], micro_index, 1)
         outputs = jnp.where(in_window, updated, outputs)
         if moment + 1 < turns:
-            full_rows = lax.all_gather(new_cols, "dp", axis=1, tiled=True)
+            e_next, v1, state_next = (lax.psum(1, "dp"), lax.axis_index("dp"), new_cols.shape[1])
+            seen = [(b, (b + 1) % e_next) for b in range(e_next)]
+            full_rows = jnp.zeros(
+                (*new_cols.shape[:1], e_next * state_next, *new_cols.shape[1 + 1 :]), new_cols.dtype
+            )
+            full_rows = lax.dynamic_update_slice_in_dim(
+                full_rows, new_cols, v1 * state_next, axis=1
+            )
+            windows = [(b, (b - 1) % e_next) for b in range(e_next)]
+            tall = e_next // 2
+            n_now = newest = new_cols
+            for j in range(1, tall + 1):
+                n_now = lax.ppermute(n_now, "dp", seen)
+                full_rows = lax.dynamic_update_slice_in_dim(
+                    full_rows, n_now, (v1 - j) % e_next * state_next, axis=1
+                )
+                if j < e_next - tall:
+                    newest = lax.ppermute(newest, "dp", windows)
+                    full_rows = lax.dynamic_update_slice_in_dim(
+                        full_rows, newest, (v1 + j) % e_next * state_next, axis=1
+                    )
             carried = passed_along(full_rows, "pipe", 1)
     return outputs
 

time: 200 us -> 191 us (0.955)
  blocking collectives: 59.6 us -> 41.1 us
  waiting for transfers between devices: 81 us -> 88.8 us
  starting transfers between devices: 13.5 us -> 17.8 us
    all_gather x2 -> x0, blocking collectives: 26.9 us -> none  [per_device(): full_rows = lax.all_gather(new_cols, 'dp', axis=1, tiled=True)]
    ppermute x0 -> x6, waiting for transfers between devices: none -> 15.3 us  [the longest x4 15.3 us: per_device(): n_now = lax.ppermute(n_now, 'dp', seen)]
    all_to_all x0 -> x1, blocking collectives: none -> 8.4 us  [per_device(): lax.all_to_all(shares, 'expert', split_axis=1, concat_axis=1, tiled=True)]
    ppermute x0 -> x6, starting transfers between devices: none -> 7.74 us  [the longest x2 7.62 us: per_device(): newest = lax.ppermute(newest, 'dp', windows)]
    all_to_all x3 -> x2, waiting for transfers between devices: 14.4 us -> 9.47 us  [per_device(): lax.all_to_all(shares, 'expert', split_axis=1, concat_axis=1, tiled=True)]
    all_to_all x3 -> x2, starting transfers between devices: 11 us -> 7.44 us  [per_device(): lax.all_to_all(shares, 'expert', split_axis=1, concat_axis=1, tiled=True)]
    reduce_scatter x3, waiting for transfers between devices: 64.7 us -> 62.2 us  [per_device(): lax.psum_scatter(lax.dot_general(down_local, hidden, (((0,), (1,)), ((),...]
  transfers between devices with their start and end apart: 8 -> 13, of which waited for: 8 -> 11; matrix products, arithmetic and copies ran while one was open for 1% -> 1% of each run, Pallas kernels for 0% -> 0%
where the time goes in v1:
time: 191 us; the launch traced here: 190 us
  waiting for transfers between devices  88.8 us (46%)
  blocking collectives  41.1 us (22%)
  starting transfers between devices  17.8 us (9%)
  matrix products  15.8 us (8%)
  between operations  13.5 us (7%)
  other arithmetic  7.68 us (4%)
  local copies, waits for them, and re-layouts  5.26 us (3%)
    reduce_scatter x3, waiting for transfers between devices, per_device(): lax.psum_scatter(lax.dot_general(down_local, hidden, (((0,), (1,)), ((),...  62.2 us
    all_to_all x3, blocking collectives, per_device(): lax.all_to_all(outgoing, 'expert', split_axis=0, concat_axis=0, tiled=True)  32.7 us
    ppermute x4, waiting for transfers between devices, per_device(): n_now = lax.ppermute(n_now, 'dp', seen)  15.3 us
    all_to_all x2, waiting for transfers between devices, per_device(): lax.all_to_all(shares, 'expert', split_axis=1, concat_axis=1, tiled=True)  9.47 us
    dot_general x3, matrix products, per_device(): lax.dot_general(down_local, hidden, (((0,), (1,)), ((), ())), preferred_e...  8.54 us
    all_to_all x1, blocking collectives, per_device(): lax.all_to_all(shares, 'expert', split_axis=1, concat_axis=1, tiled=True)  8.4 us
    ppermute x2, starting transfers between devices, per_device(): newest = lax.ppermute(newest, 'dp', windows)  7.62 us
    all_to_all x2, starting transfers between devices, per_device(): lax.all_to_all(shares, 'expert', split_axis=1, concat_axis=1, tiled=True)  7.44 us
  transfers between devices with their start and end apart: 13, of which 11 were waited for; matrix products, arithmetic and copies ran while one was open for 1% of the time, Pallas kernels for 0%

profile of v1, /device:TPU:0, one launch (start us, length us, event | category | flops | bytes accessed | tf_op | source)
XLA Modules:
  0.0 189.9 jit_solution(10063091718997875540)
XLA Ops:
  10.1 12.1 %all_to_all.30 = bf16[4,16,3072]{2,1,0:T(8,128)(2,1)S(1)} all-to-all(bf16[4,16,3072]{2,1,0:T(8,128)(2,1)S(1)} %bitcast.104), channel_id=1, replica_groups=mesh['dp'=4,'pipe'=2,'expert'=4] {'expert'}, dimensions={0} | all-to-all | bytes 786432 | tf_op jit(solution)/shard_map/all_to_all | solution.py:62
  23.2 1.5 convolution_multiply_fusion.5
  24.8 2.8 %convolution_bitcast_fusion.2 = f32[3072,64]{0,1:T(8,128)} fusion(bf16[64,3072]{1,0:T(8,128)(2,1)} %bitcast.99, bf16[1,1,176,3072]{3,2,1,0:T(8,128)(2,1)S(1)} %copy-done, bf16[1,1,3072,176]{2,3,1,0:T(8,128)(2,1)S(1)} %copy-done.2, f32[64,176]{1,0:T(8,128)S(1)} %convolution_multiply_fusion.5, f32[64]{0:T(128)S(1)} %rsqrt.34), kind=kOutput, calls=%fused_computation.2 | convolution fusion | flops 138490880 | bytes 3387648 | tf_op jit(solution)/shard_map/dot_general | solution.py:72
  28.8 22.1 %reduce-scatter.4.cloned.1.call-done = f32[768,64]{0,1:T(8,128)} async-done(((f32[3072,64]{0,1:T(8,128)}), f32[768,64]{0,1:T(8,128)}) %reduce-scatter.4.cloned.1.call-update) | async-done | bytes 196624 | tf_op jit(solution)/shard_map/reduce_scatter | solution.py:71
  50.8 1.6 convert_element_type.101
  52.4 3.7 %all-to-all-start.1 = ((bf16[768,4,16]{0,2,1:T(8,128)(2,1)}), bf16[768,4,16]{0,2,1:T(8,128)(2,1)S(1)}, u32[]{:S(2)}, u32[]{:S(2)}) async-start(bf16[768,4,16]{0,2,1:T(8,128)(2,1)} %bitcast.110), calls=%async_computation.2 | async-start | bytes 196608 | tf_op jit(solution)/shard_map/all_to_all | solution.py:80
  56.4 4.6 %all-to-all-done.1 = bf16[768,4,16]{0,2,1:T(8,128)(2,1)S(1)} async-done(((bf16[768,4,16]{0,2,1:T(8,128)(2,1)}), bf16[768,4,16]{0,2,1:T(8,128)(2,1)S(1)}, u32[]{:S(2)}, u32[]{:S(2)}) %all-to-all-start.1) | async-done | bytes 98336 | tf_op jit(solution)/shard_map/all_to_all | solution.py:80
  61.3 3.8 %collective-permute-start.1 = (bf16[24,768]{1,0:T(8,128)(2,1)S(1)}, bf16[24,768]{1,0:T(8,128)(2,1)S(1)}, u32[]{:S(2)}, u32[]{:S(2)}) collective-permute-start(bf16[24,768]{1,0:T(8,128)(2,1)S(1)} %get-tuple-element.20), channel_id=1, source_target_pairs={{0,24},{8,0},{16,8},{24,16},{1,25},{9,1},{17,9},{25,17},{2,26},{10... | collective-permute-start | bytes 110600 | tf_op jit(solution)/shard_map/ppermute | solution.py:111
  65.1 1.9 collective-permute-done
  67.1 5.7 %collective-permute-done.2 = bf16[24,768]{1,0:T(8,128)(2,1)S(1)} collective-permute-done((bf16[24,768]{1,0:T(8,128)(2,1)S(1)}, bf16[24,768]{1,0:T(8,128)(2,1)S(1)}, u32[]{:S(2)}, u32[]{:S(2)}) %collective-permute-start.2) | collective-permute-done | bytes 36896 | tf_op jit(solution)/shard_map/ppermute | solution.py:106
  76.3 10.3 %all_to_all.31 = bf16[4,16,3072]{2,1,0:T(8,128)(2,1)S(1)} all-to-all(bf16[4,16,3072]{2,1,0:T(8,128)(2,1)S(1)} %bitcast.105), channel_id=1, replica_groups=mesh['dp'=4,'pipe'=2,'expert'=4] {'expert'}, dimensions={0} | all-to-all | bytes 786432 | tf_op jit(solution)/shard_map/all_to_all | solution.py:62
  89.1 2.8 %convolution_bitcast_fusion.1 = f32[3072,64]{0,1:T(8,128)} fusion(bf16[64,3072]{1,0:T(8,128)(2,1)} %bitcast.101, bf16[1,1,176,3072]{3,2,1,0:T(8,128)(2,1)S(1)} %copy-done, bf16[1,1,3072,176]{2,3,1,0:T(8,128)(2,1)S(1)} %copy-done.2, f32[64,176]{1,0:T(8,128)S(1)} %convolution_multiply_fusion.3, f32[64]{0:T(128)S(1)} %rsqrt.36), kind=kOutput, calls=%fused_computation.1 | convolution fusion | flops 138490880 | bytes 3387648 | tf_op jit(solution)/shard_map/dot_general | solution.py:72
  92.0 20.1 %reduce-scatter.6.cloned.1.call-done = f32[768,64]{0,1:T(8,128)} async-done(((f32[3072,64]{0,1:T(8,128)}), f32[768,64]{0,1:T(8,128)}) %reduce-scatter.6.cloned.1.call-update) | async-done | bytes 196624 | tf_op jit(solution)/shard_map/reduce_scatter | solution.py:71
  113.1 8.4 %all_to_all.32 = bf16[768,4,16]{0,2,1:T(8,128)(2,1)S(1)} all-to-all(bf16[768,4,16]{0,2,1:T(8,128)(2,1)S(1)} %bitcast.111), channel_id=1, replica_groups=mesh['dp'=4,'pipe'=2,'expert'=4] {'expert'}, dimensions={1} | all-to-all | bytes 196608 | tf_op jit(solution)/shard_map/all_to_all | solution.py:80
  121.7 3.8 %collective-permute-start.5 = (bf16[24,768]{1,0:T(8,128)(2,1)S(1)}, bf16[24,768]{1,0:T(8,128)(2,1)S(1)}, u32[]{:S(2)}, u32[]{:S(2)}) collective-permute-start(bf16[24,768]{1,0:T(8,128)(2,1)S(1)} %get-tuple-element.12), channel_id=1, source_target_pairs={{0,24},{8,0},{16,8},{24,16},{1,25},{9,1},{17,9},{25,17},{2,26},{10... | collective-permute-start | bytes 110600 | tf_op jit(solution)/shard_map/ppermute | solution.py:111
  125.5 1.9 %collective-permute-done.4 = bf16[24,768]{1,0:T(8,128)(2,1)S(1)} collective-permute-done((bf16[24,768]{1,0:T(8,128)(2,1)S(1)}, bf16[24,768]{1,0:T(8,128)(2,1)S(1)}, u32[]{:S(2)}, u32[]{:S(2)}) %collective-permute-start.4) | collective-permute-done | bytes 36896 | tf_op jit(solution)/shard_map/ppermute | solution.py:106
  127.5 5.7 %collective-permute-done.6 = bf16[24,768]{1,0:T(8,128)(2,1)S(1)} collective-permute-done((bf16[24,768]{1,0:T(8,128)(2,1)S(1)}, bf16[24,768]{1,0:T(8,128)(2,1)S(1)}, u32[]{:S(2)}, u32[]{:S(2)}) %collective-permute-start.6) | collective-permute-done | bytes 36896 | tf_op jit(solution)/shard_map/ppermute | solution.py:106
  135.8 10.3 %all_to_all.33 = bf16[4,16,3072]{2,1,0:T(8,128)(2,1)S(1)} all-to-all(bf16[4,16,3072]{2,1,0:T(8,128)(2,1)S(1)} %bitcast.106), channel_id=1, replica_groups=mesh['dp'=4,'pipe'=2,'expert'=4] {'expert'}, dimensions={0} | all-to-all | bytes 786432 | tf_op jit(solution)/shard_map/all_to_all | solution.py:62
  148.6 2.8 %convolution_bitcast_fusion = f32[3072,64]{0,1:T(8,128)} fusion(bf16[64,3072]{1,0:T(8,128)(2,1)} %bitcast.103, bf16[1,1,176,3072]{3,2,1,0:T(8,128)(2,1)S(1)} %copy-done, bf16[1,1,3072,176]{2,3,1,0:T(8,128)(2,1)S(1)} %copy-done.2, f32[64,176]{1,0:T(8,128)S(1)} %convolution_multiply_fusion.1, f32[64]{0:T(128)S(1)} %rsqrt.38), kind=kOutput, calls=%fused_computation | convolution fusion | flops 138490880 | bytes 3387648 | tf_op jit(solution)/shard_map/dot_general | solution.py:72
  151.5 20.1 %reduce-scatter.8.cloned.1.call-done = f32[768,64]{0,1:T(8,128)} async-done(((f32[3072,64]{0,1:T(8,128)}), f32[768,64]{0,1:T(8,128)}) %reduce-scatter.8.cloned.1.call-update) | async-done | bytes 196624 | tf_op jit(solution)/shard_map/reduce_scatter | solution.py:71
  171.6 1.6 convert_element_type.119
  173.2 3.7 %all-to-all-start.5 = ((bf16[768,4,16]{0,2,1:T(8,128)(2,1)}), bf16[768,4,16]{0,2,1:T(8,128)(2,1)S(1)}, u32[]{:S(2)}, u32[]{:S(2)}) async-start(bf16[768,4,16]{0,2,1:T(8,128)(2,1)} %bitcast.27), calls=%async_computation.8 | async-start | bytes 196608 | tf_op jit(solution)/shard_map/all_to_all | solution.py:80
  176.9 4.9 %all-to-all-done.5 = bf16[768,4,16]{0,2,1:T(8,128)(2,1)S(1)} async-done(((bf16[768,4,16]{0,2,1:T(8,128)(2,1)}), bf16[768,4,16]{0,2,1:T(8,128)(2,1)S(1)}, u32[]{:S(2)}, u32[]{:S(2)}) %all-to-all-start.5) | async-done | bytes 98336 | tf_op jit(solution)/shard_map/all_to_all | solution.py:80
  181.9 1.6 fusion.37
  (95 shorter events, 18.6 us)
Async XLA Ops:
  6.5 18.2 %copy-start = (bf16[1,1,176,3072]{3,2,1,0:T(8,128)(2,1)S(1)}, bf16[1,1,176,3072]{3,2,1,0:T(8,128)(2,1)}, u32[]{:S(2)}) copy-start(bf16[1,1,176,3072]{3,2,1,0:T(8,128)(2,1)} %param.11) | copy-start | bytes 3244036
  6.5 44.3 %reduce-scatter.4.cloned.1.call-start = ((), (), s32[]{:S(2)}) async-start(), calls=%async_computation.9 | async-start | bytes 983040 | tf_op jit(solution)/shard_map/reduce_scatter | solution.py:71
  7.6 15.6 %copy-start.1 = (bf16[1,1,3072,176]{2,3,1,0:T(8,128)(2,1)S(1)}, bf16[1,1,3072,176]{2,3,1,0:T(8,128)(2,1)}, u32[]{:S(2)}) copy-start(bf16[1,1,3072,176]{2,3,1,0:T(8,128)(2,1)} %param.9) | copy-start | bytes 3244036
  22.2 0.7 copy-start.3
  23.0 1.8 copy-start.2
  52.4 8.7 %all-to-all-start.1 = ((bf16[768,4,16]{0,2,1:T(8,128)(2,1)}), bf16[768,4,16]{0,2,1:T(8,128)(2,1)S(1)}, u32[]{:S(2)}, u32[]{:S(2)}) async-start(bf16[768,4,16]{0,2,1:T(8,128)(2,1)} %bitcast.110), calls=%async_computation.2 | async-start | bytes 196608 | tf_op jit(solution)/shard_map/all_to_all | solution.py:80
  56.1 56.0 %reduce-scatter.6.cloned.1.call-start = ((), (), s32[]{:S(2)}) async-start(), calls=%async_computation.10 | async-start | bytes 983040 | tf_op jit(solution)/shard_map/reduce_scatter | solution.py:71
  61.2 14.8 %copy-start.7 = (bf16[1,2,24,768]{3,2,1,0:T(8,128)(2,1)}, bf16[1,2,24,768]{3,2,1,0:T(8,128)(2,1)S(1)}, u32[]{:S(2)}) copy-start(bf16[1,2,24,768]{3,2,1,0:T(8,128)(2,1)S(1)} %get-tuple-element.19) | copy-start | bytes 221188
  61.2 5.8 %collective-permute-start = (bf16[24,768]{1,0:T(8,128)(2,1)S(1)}, bf16[24,768]{1,0:T(8,128)(2,1)S(1)}, u32[]{:S(2)}, u32[]{:S(2)}) collective-permute-start(bf16[24,768]{1,0:T(8,128)(2,1)S(1)} %get-tuple-element.20), channel_id=1, source_target_pairs={{0,8},{8,16},{16,24},{24,0},{1,9},{9,17},{17,25},{25,1},{2,10},{10... | collective-permute-start | bytes 110600 | tf_op jit(solution)/shard_map/ppermute | solution.py:106
  61.3 5.8 %collective-permute-start.1 = (bf16[24,768]{1,0:T(8,128)(2,1)S(1)}, bf16[24,768]{1,0:T(8,128)(2,1)S(1)}, u32[]{:S(2)}, u32[]{:S(2)}) collective-permute-start(bf16[24,768]{1,0:T(8,128)(2,1)S(1)} %get-tuple-element.20), channel_id=1, source_target_pairs={{0,24},{8,0},{16,8},{24,16},{1,25},{9,1},{17,9},{25,17},{2,26},{10... | collective-permute-start | bytes 110600 | tf_op jit(solution)/shard_map/ppermute | solution.py:111
  67.0 5.8 %collective-permute-start.2 = (bf16[24,768]{1,0:T(8,128)(2,1)S(1)}, bf16[24,768]{1,0:T(8,128)(2,1)S(1)}, u32[]{:S(2)}, u32[]{:S(2)}) collective-permute-start(bf16[24,768]{1,0:T(8,128)(2,1)S(1)} %collective-permute-done), channel_id=1, source_target_pairs={{0,8},{8,16},{16,24},{24,0},{1,9},{9,17},{17,25},{25,1},{2,10},{10... | collective-permute-start | bytes 110600 | tf_op jit(solution)/shard_map/ppermute | solution.py:106
  72.8 2.3 %collective-permute-start.3 = (bf16[24,3072]{1,0:T(8,128)(2,1)S(1)}, bf16[24,3072]{1,0:T(8,128)(2,1)S(1)}, u32[]{:S(2)}, u32[]{:S(2)}) collective-permute-start(bf16[24,3072]{1,0:T(8,128)(2,1)S(1)} %constant_dynamic-update-slice_fusion.4), channel_id=1, source_target_pairs={{0,4},{1,5},{2,6},{3,7},{8,12},{9,13},{10,14},{11,15},{16,20},{17,... | collective-permute-start | bytes 442376 | tf_op jit(solution)/shard_map/ppermute | solution.py:13
  86.6 0.7 copy-start.4
  92.0 79.7 %reduce-scatter.8.cloned.1.call-start = ((), (), s32[]{:S(2)}) async-start(), calls=%async_computation.11 | async-start | bytes 983040 | tf_op jit(solution)/shard_map/reduce_scatter | solution.py:71
  112.1 23.4 %copy-start.6 = (bf16[2,24,3072]{2,1,0:T(8,128)(2,1)S(1)}, bf16[2,24,3072]{2,1,0:T(8,128)(2,1)}, u32[]{:S(2)}) copy-start(bf16[2,24,3072]{2,1,0:T(8,128)(2,1)} %param.6) | copy-start | bytes 884740
  121.7 5.8 %collective-permute-start.4 = (bf16[24,768]{1,0:T(8,128)(2,1)S(1)}, bf16[24,768]{1,0:T(8,128)(2,1)S(1)}, u32[]{:S(2)}, u32[]{:S(2)}) collective-permute-start(bf16[24,768]{1,0:T(8,128)(2,1)S(1)} %get-tuple-element.12), channel_id=1, source_target_pairs={{0,8},{8,16},{16,24},{24,0},{1,9},{9,17},{17,25},{25,1},{2,10},{10... | collective-permute-start | bytes 110600 | tf_op jit(solution)/shard_map/ppermute | solution.py:106
  121.7 5.8 %collective-permute-start.5 = (bf16[24,768]{1,0:T(8,128)(2,1)S(1)}, bf16[24,768]{1,0:T(8,128)(2,1)S(1)}, u32[]{:S(2)}, u32[]{:S(2)}) collective-permute-start(bf16[24,768]{1,0:T(8,128)(2,1)S(1)} %get-tuple-element.12), channel_id=1, source_target_pairs={{0,24},{8,0},{16,8},{24,16},{1,25},{9,1},{17,9},{25,17},{2,26},{10... | collective-permute-start | bytes 110600 | tf_op jit(solution)/shard_map/ppermute | solution.py:111
  127.5 5.8 %collective-permute-start.6 = (bf16[24,768]{1,0:T(8,128)(2,1)S(1)}, bf16[24,768]{1,0:T(8,128)(2,1)S(1)}, u32[]{:S(2)}, u32[]{:S(2)}) collective-permute-start(bf16[24,768]{1,0:T(8,128)(2,1)S(1)} %collective-permute-done.4), channel_id=1, source_target_pairs={{0,8},{8,16},{16,24},{24,0},{1,9},{9,17},{17,25},{25,1},{2,10},{10... | collective-permute-start | bytes 110600 | tf_op jit(solution)/shard_map/ppermute | solution.py:106
  133.2 2.3 %collective-permute-start.7 = (bf16[24,3072]{1,0:T(8,128)(2,1)S(1)}, bf16[24,3072]{1,0:T(8,128)(2,1)S(1)}, u32[]{:S(2)}, u32[]{:S(2)}) collective-permute-start(bf16[24,3072]{1,0:T(8,128)(2,1)S(1)} %constant_dynamic-update-slice_fusion), channel_id=1, source_target_pairs={{0,4},{1,5},{2,6},{3,7},{8,12},{9,13},{10,14},{11,15},{16,20},{17,... | collective-permute-start | bytes 442376 | tf_op jit(solution)/shard_map/ppermute | solution.py:13
  146.2 0.7 copy-start.5
  151.5 25.4 %copy-start.8 = (bf16[1,2,24,768]{3,2,1,0:T(8,128)(2,1)S(1)}, bf16[1,2,24,768]{3,2,1,0:T(8,128)(2,1)}, u32[]{:S(2)}) copy-start(bf16[1,2,24,768]{3,2,1,0:T(8,128)(2,1)} %copy-done.7) | copy-start | bytes 221188
  173.2 8.7 %all-to-all-start.5 = ((bf16[768,4,16]{0,2,1:T(8,128)(2,1)}), bf16[768,4,16]{0,2,1:T(8,128)(2,1)S(1)}, u32[]{:S(2)}, u32[]{:S(2)}) async-start(bf16[768,4,16]{0,2,1:T(8,128)(2,1)} %bitcast.27), calls=%async_computation.8 | async-start | bytes 196608 | tf_op jit(solution)/shard_map/all_to_all | solution.py:80
  176.9 4.9 %copy-start.9 = (bf16[1,2,24,768]{3,2,1,0:T(8,128)(2,1)}, bf16[1,2,24,768]{3,2,1,0:T(8,128)(2,1)S(1)}, u32[]{:S(2)}) copy-start(bf16[1,2,24,768]{3,2,1,0:T(8,128)(2,1)S(1)} %fusion.38) | copy-start | bytes 221188
Sparse Core Ops, SparseCore 0:
  27.8 23.0 reduce-scatter.3
  92.1 19.9 reduce-scatter.5
  151.6 19.9 reduce-scatter.7
